TPU v7x, 256 devices: a whole 4x4x8 slice. The times are simulated.
256 devices in a mesh: pix: 32 (over z, x), feat: 8 (over y, core).
Axes of the slice: x: 4, y: 4, z: 8, core: 2. Of those that a mesh axis runs over, the one named last changes fastest.
Arguments:
- mass_bin: int32 [262144, 256], P(('pix', 'feat')), may hold values from 0 to 255
- mobility_bin: int32 [262144, 256], P(('pix', 'feat')), may hold values from 0 to 15
- intensity: bfloat16 [262144, 256], P(('pix', 'feat')), may hold values from 10 to 4000, as said below
- basis_init: float32 [262144, 64], P(('pix', 'feat')), may hold values from 0.1 to 1
- profile_init: float32 [64, 4096], P(None, 'feat'), may hold values from 0.1 to 1
Outputs:
- basis: float32 [262144, 64], P(('pix', 'feat'))
- profiles: float32 [64, 4096], P(None, 'feat')
Inputs may be any that keep to these rules, and one draw needn't show every extreme that they name: `intensity`: positive peak intensities.
All inputs are finite; a program needn't handle non-finite values.
Results may differ from a plain program's by a relative error of at most 0.00045.
Values may be sent and summed in bfloat16 or wider, within the bound.
No kernel may reach another device: no remote copies, remote signals or barrier semaphores. Data moves between devices by JAX's collectives and lax.ppermute only.
A program may use at most 64 MiB of HBM per device.

v0:
```python
import math
import jax
import jax.numpy as jnp
from jax import lax
from jax.sharding import PartitionSpec as P

MZ = 256
MOB = 16
PEAKS = 256
ITERS = 2
EPS = 1e-06


def bin_block(args):
    mass, mobility, weight = args
    mass_hot = (mass[:, :, None] == jnp.arange(MZ, dtype=jnp.int32)[None, None, :]).astype(
        jnp.bfloat16
    ) * weight[:, :, None]
    mobility_hot = (mobility[:, :, None] == jnp.arange(MOB, dtype=jnp.int32)[None, None, :]).astype(
        jnp.bfloat16
    )
    dense = jnp.einsum("pkb,pkm->pbm", mobility_hot, mass_hot, preferred_element_type=jnp.float32)
    return dense.reshape(mass.shape[0], MZ * MOB).astype(jnp.bfloat16)


def local(mass_bin, mobility_bin, intensity, basis_init, profile_init):
    rows = mass_bin.shape[0]
    block = math.gcd(rows, 32)
    count = rows // block
    spectra = lax.map(
        bin_block,
        (
            mass_bin.reshape(count, block, PEAKS),
            mobility_bin.reshape(count, block, PEAKS),
            intensity.reshape(count, block, PEAKS),
        ),
    )
    spectra = spectra.reshape(rows, MZ * MOB)
    highest = lax.Precision.HIGHEST
    basis, profiles = (basis_init, profile_init)
    for step in range(ITERS):
        partial_h = lax.dot_general(
            basis.astype(jnp.bfloat16),
            spectra,
            (((0,), (0,)), ((), ())),
            preferred_element_type=jnp.float32,
        )
        partial_gram = lax.dot_general(
            basis,
            basis,
            (((0,), (0,)), ((), ())),
            precision=highest,
            preferred_element_type=jnp.float32,
        )
        shared = lax.psum_scatter(partial_h, "feat", scatter_dimension=1, tiled=True)
        numer_h = lax.psum(shared, "pix")
        gram_w = lax.psum(partial_gram, ("pix", "feat"))
        profiles = (
            profiles
            * numer_h
            / (
                jnp.dot(gram_w, profiles, precision=highest, preferred_element_type=jnp.float32)
                + EPS
            )
        )
        numer_w = lax.dot_general(
            spectra,
            lax.all_gather(profiles.astype(jnp.bfloat16), "feat", axis=1, tiled=True),
            (((1,), (1,)), ((), ())),
            preferred_element_type=jnp.float32,
        )
        local_gram = lax.dot_general(
            profiles,
            profiles,
            (((1,), (1,)), ((), ())),
            precision=highest,
            preferred_element_type=jnp.float32,
        )
        gram_h = lax.psum(local_gram, "feat")
        basis = (
            basis
            * numer_w
            / (jnp.dot(basis, gram_h, precision=highest, preferred_element_type=jnp.float32) + EPS)
        )
    return (basis, profiles)


def solution(mesh):
    return jax.shard_map(
        local,
        mesh=mesh,
        in_specs=(
            P(("pix", "feat"), None),
            P(("pix", "feat"), None),
            P(("pix", "feat"), None),
            P(("pix", "feat"), None),
            P(None, "feat"),
        ),
        out_specs=(P(("pix", "feat"), None), P(None, "feat")),
        check_vma=False,
    )
```

profile of v0, /device:TPU:2, one launch (start us, length us, event | category | flops | bytes accessed | tf_op | source)
XLA Modules:
  0.0 668.2 jit_solution(15157433333801755827)
XLA Ops:
  7.2 192.9 %while.10 = (s32[]{:T(128)}, bf16[32,32,4096]{2,1,0:T(8,128)(2,1)}, s32[32,32,256]{2,1,0:T(8,128)}, s32[32,32,256]{2,1,0:T(8,128)}, bf16[32,32,256]{2,1,0:T(8,128)(2,1)}, /*index=5*/s32[]{:T(128)}) while((s32[]{:T(128)}, bf16[32,32,4096]{2,1,0:T(8,128)(2,1)}, s32[32,32,256]{2,1,0:T(8,128)}, s32[32,32,256]{2,1,0:T(8,128)}, ...), condition=%wide.region_1.2_spmd, body=%wide.region_0.1_spmd.sunk | while | flops 71565312 | bytes 1557069 | solution.py:30
  8.8 3.7 fusion.50
  14.8 3.7 fusion.50
  20.8 3.7 fusion.50
  26.8 3.7 fusion.50
  32.9 3.7 fusion.50
  38.9 3.7 fusion.50
  44.9 3.7 fusion.50
  51.0 3.7 fusion.50
  57.0 3.7 fusion.50
  63.0 3.7 fusion.50
  69.0 3.7 fusion.50
  75.1 3.7 fusion.50
  81.1 3.7 fusion.50
  87.1 3.7 fusion.50
  93.2 3.7 fusion.50
  99.2 3.7 fusion.50
  105.2 3.7 fusion.50
  111.2 3.7 fusion.50
  117.2 3.7 fusion.50
  123.3 3.7 fusion.50
  129.3 3.7 fusion.50
  135.3 3.7 fusion.50
  141.4 3.7 fusion.50
  147.4 3.7 fusion.50
  153.4 3.7 fusion.50
  159.4 3.7 fusion.50
  165.5 3.7 fusion.50
  171.5 3.7 fusion.50
  177.5 3.7 fusion.50
  183.6 3.7 fusion.50
  189.6 3.7 fusion.50
  195.6 3.7 fusion.50
  200.1 6.1 convolution_bitcast_fusion
  206.2 37.5 %reduce-scatter.3.cloned.1.call-done = f32[64,512]{1,0:T(8,128)} async-done(((f32[64,4096]{1,0:T(8,128)}), f32[64,512]{1,0:T(8,128)}) %reduce-scatter.3.cloned.1.call-update) | async-done | bytes 131088 | tf_op jit(solution)/shard_map/reduce_scatter | solution.py:55
  244.2 74.5 %psum.43 = f32[64,64]{1,0:T(8,128)S(1)} all-reduce(f32[64,64]{1,0:T(8,128)S(1)} %fusion.21), channel_id=1, replica_groups=mesh['pix'=32,'feat'=8] {'pix','feat'}, use_global_device_ids=true, to_apply=%region_4.5 | all-reduce | flops 4096 | bytes 32768 | tf_op jit(solution)/shard_map/psum | solution.py:57
  318.7 68.1 %all-reduce.3.cloned.1.call-done = f32[64,512]{1,0:T(8,128)} async-done(((f32[64,512]{1,0:T(8,128)}), f32[64,512]{1,0:T(8,128)}) %all-reduce.3.cloned.1.call-update) | async-done | bytes 131088 | tf_op jit(solution)/shard_map/psum | solution.py:56
  386.8 1.2 fusion.19
  388.0 13.5 %all_gather.6 = bf16[64,4096]{1,0:T(8,128)(2,1)S(1)} all-gather(bf16[64,512]{1,0:T(8,128)(2,1)S(1)} %get-tuple-element.42), channel_id=1, replica_groups=mesh['pix'=32,'feat'=8] {'feat'}, dimensions={1}, use_global_device_ids=true | all-gather | bytes 589824 | tf_op jit(solution)/shard_map/all_gather | solution.py:68
  401.5 6.0 convolution_multiply_fusion.1
  407.8 25.8 %psum.44 = f32[64,64]{1,0:T(8,128)S(1)} all-reduce(f32[64,64]{1,0:T(8,128)S(1)} %fusion.22), channel_id=1, replica_groups=mesh['pix'=32,'feat'=8] {'feat'}, use_global_device_ids=true, to_apply=%region_5.6 | all-reduce | flops 4096 | bytes 32768 | tf_op jit(solution)/shard_map/psum | solution.py:79
  434.0 6.0 fusion.16
  440.1 30.4 %reduce-scatter.5.cloned.1.call-done = f32[64,512]{1,0:T(8,128)} async-done(((f32[64,4096]{1,0:T(8,128)}), f32[64,512]{1,0:T(8,128)}) %reduce-scatter.5.cloned.1.call-update) | async-done | bytes 131088 | tf_op jit(solution)/shard_map/reduce_scatter | solution.py:55
  470.8 74.4 %psum.46 = f32[64,64]{1,0:T(8,128)S(1)} all-reduce(f32[64,64]{1,0:T(8,128)S(1)} %fusion.23), channel_id=1, replica_groups=mesh['pix'=32,'feat'=8] {'pix','feat'}, use_global_device_ids=true, to_apply=%region_8.9 | all-reduce | flops 4096 | bytes 32768 | tf_op jit(solution)/shard_map/psum | solution.py:57
  545.2 68.6 %all-reduce.5.cloned.1.call-done = f32[64,512]{1,0:T(8,128)} async-done(((f32[64,512]{1,0:T(8,128)}), f32[64,512]{1,0:T(8,128)}) %all-reduce.5.cloned.1.call-update) | async-done | bytes 131088 | tf_op jit(solution)/shard_map/psum | solution.py:56
  615.0 13.4 %all_gather.7 = bf16[64,4096]{1,0:T(8,128)(2,1)S(1)} all-gather(bf16[64,512]{1,0:T(8,128)(2,1)S(1)} %get-tuple-element.44), channel_id=1, replica_groups=mesh['pix'=32,'feat'=8] {'feat'}, dimensions={1}, use_global_device_ids=true | all-gather | bytes 589824 | tf_op jit(solution)/shard_map/all_gather | solution.py:68
  628.5 6.0 convolution_multiply_fusion
  634.8 25.8 %psum.47 = f32[64,64]{1,0:T(8,128)S(1)} all-reduce(f32[64,64]{1,0:T(8,128)S(1)} %fusion.24), channel_id=1, replica_groups=mesh['pix'=32,'feat'=8] {'feat'}, use_global_device_ids=true, to_apply=%region_9.10 | all-reduce | flops 4096 | bytes 32768 | tf_op jit(solution)/shard_map/psum | solution.py:79
  (150 shorter events, 79.7 us)
Async XLA Ops:
  7.2 236.6 %reduce-scatter.3.cloned.1.call-start = ((), (), s32[]{:S(2)}) async-start(), calls=%async_computation.2 | async-start | bytes 1179648 | tf_op jit(solution)/shard_map/reduce_scatter | solution.py:55
  7.2 192.9 %copy-start = (f32[1024,64]{0,1:T(8,128)S(1)}, f32[1024,64]{0,1:T(8,128)}, u32[]{:S(2)}) copy-start(f32[1024,64]{0,1:T(8,128)} %param.10) | copy-start | bytes 786436
  200.1 186.7 %copy-start.2 = (f32[64,512]{1,0:T(8,128)S(1)}, f32[64,512]{1,0:T(8,128)}, u32[]{:S(2)}) copy-start(f32[64,512]{1,0:T(8,128)} %param.11) | copy-start | bytes 393220
  206.2 180.6 %all-reduce.3.cloned.1.call-start = ((), (), s32[]{:S(2)}) async-start(), calls=%async_computation.3 | async-start | bytes 262144 | tf_op jit(solution)/shard_map/psum | solution.py:56
  243.8 226.7 %reduce-scatter.5.cloned.1.call-start = ((), (), s32[]{:S(2)}) async-start(), calls=%async_computation.4 | async-start | bytes 1179648 | tf_op jit(solution)/shard_map/reduce_scatter | solution.py:55
  440.0 173.8 %all-reduce.5.cloned.1.call-start = ((), (), s32[]{:S(2)}) async-start(), calls=%async_computation.5 | async-start | bytes 262144 | tf_op jit(solution)/shard_map/psum | solution.py:56
  615.0 46.7 %copy-start.1 = (f32[64,512]{1,0:T(8,128)}, f32[64,512]{1,0:T(8,128)S(1)}, u32[]{:S(2)}) copy-start(f32[64,512]{1,0:T(8,128)S(1)} %get-tuple-element.45) | copy-start | bytes 393220
Sparse Core Ops, SparseCore 0:
  206.3 37.3 reduce-scatter.2
  247.2 139.5 all-reduce.2
  440.1 30.2 reduce-scatter.4
  474.1 139.6 all-reduce.4
where the time goes:
time: 673 us; the launch traced here: 668 us
  blocking collectives  227 us (34%)
  waiting for transfers between devices  205 us (30%)
  matrix products  146 us (22%)
  local copies, waits for them, and re-layouts  75.5 us (11%)
  between operations  13.8 us (2%)
    psum x2, blocking collectives, local(): gram_w = lax.psum(partial_gram, ('pix', 'feat'))  149 us
    psum x2, waiting for transfers between devices, local(): numer_h = lax.psum(shared, 'pix')  137 us
    dot_general x32, matrix products, bin_block(): jnp.einsum('pkb,pkm->pbm', mobility_hot, mass_hot, preferred_element_type...  117 us
    reduce_scatter x2, waiting for transfers between devices, local(): lax.psum_scatter(partial_h, 'feat', scatter_dimension=1, tiled=True)  67.8 us
    psum x2, blocking collectives, local(): gram_h = lax.psum(local_gram, 'feat')  51.6 us
    all_gather x2, blocking collectives, local(): lax.all_gather(profiles.astype(jnp.bfloat16), 'feat', axis=1, tiled=True)  26.9 us
    eq x32, local copies, waits for them, and re-layouts, bin_block(): mass[:, :, None] == jnp.arange(MZ, dtype=jnp.int32)[None, None, :]  25 us
    dynamic_update_slice x32, local copies, waits for them, and re-layouts, local(): lax.map(bin_block, (mass_bin.reshape(count, block, PEAKS), mobility_bin.r...  23.4 us
  transfers between devices with their start and end apart: 4, of which 4 were waited for; matrix products, arithmetic and copies ran while one was open for 0% of the time, Pallas kernels for 0%

commit v1 on v0

--- a/solution.py
+++ b/solution.py
@@ -54,7 +54,7 @@
         )
         shared = lax.psum_scatter(partial_h, "feat", scatter_dimension=1, tiled=True)
         numer_h = lax.psum(shared, "pix")
-        gram_w = lax.psum(partial_gram, ("pix", "feat"))
+        gram_w = lax.psum(lax.psum(partial_gram, "pix"), "feat")
         profiles = (
             profiles
             * numer_h

time: 673 us -> 712 us (1.058)
  blocking collectives: 227 us -> 397 us
  waiting for transfers between devices: 205 us -> 70.8 us
    psum x2 -> x4, blocking collectives: 149 us -> 324 us  [local(): gram_w = lax.psum(lax.psum(partial_gram, 'pix'), 'feat')]
    psum x2, waiting for transfers between devices: 137 us -> 0.01 us  [local(): numer_h = lax.psum(shared, 'pix')]
  transfers between devices with their start and end apart: 4 -> 4, of which waited for: 4 -> 2; matrix products, arithmetic and copies ran while one was open for 0% -> 0% of each run, Pallas kernels for 0% -> 0%
where the time goes in v1:
time: 712 us; the launch traced here: 704 us
  blocking collectives  397 us (56%)
  matrix products  146 us (21%)
  local copies, waits for them, and re-layouts  75.5 us (11%)
  waiting for transfers between devices  70.8 us (10%)
  between operations  13.8 us (2%)
    psum x4, blocking collectives, local(): gram_w = lax.psum(lax.psum(partial_gram, 'pix'), 'feat')  324 us
    dot_general x32, matrix products, bin_block(): jnp.einsum('pkb,pkm->pbm', mobility_hot, mass_hot, preferred_element_type...  117 us
    reduce_scatter x2, waiting for transfers between devices, local(): lax.psum_scatter(partial_h, 'feat', scatter_dimension=1, tiled=True)  70.8 us
    psum x2, blocking collectives, local(): gram_h = lax.psum(local_gram, 'feat')  47.6 us
    all_gather x2, blocking collectives, local(): lax.all_gather(profiles.astype(jnp.bfloat16), 'feat', axis=1, tiled=True)  26.2 us
    eq x32, local copies, waits for them, and re-layouts, bin_block(): mass[:, :, None] == jnp.arange(MZ, dtype=jnp.int32)[None, None, :]  25 us
    dynamic_update_slice x32, local copies, waits for them, and re-layouts, local(): lax.map(bin_block, (mass_bin.reshape(count, block, PEAKS), mobility_bin.r...  23.4 us
    mul x32, local copies, waits for them, and re-layouts, bin_block(): (mass[:, :, None] == jnp.arange(MZ, dtype=jnp.int32)[None, None, :]).asty...  23 us
  transfers between devices with their start and end apart: 4, of which 2 were waited for; matrix products, arithmetic and copies ran while one was open for 0% of the time, Pallas kernels for 0%

profile of v1, /device:TPU:2, one launch (start us, length us, event | category | flops | bytes accessed | tf_op | source)
XLA Modules:
  0.0 704.4 jit_solution(3100505389470967569)
XLA Ops:
  7.2 192.9 %while.10 = (s32[]{:T(128)}, bf16[32,32,4096]{2,1,0:T(8,128)(2,1)}, s32[32,32,256]{2,1,0:T(8,128)}, s32[32,32,256]{2,1,0:T(8,128)}, bf16[32,32,256]{2,1,0:T(8,128)(2,1)}, /*index=5*/s32[]{:T(128)}) while((s32[]{:T(128)}, bf16[32,32,4096]{2,1,0:T(8,128)(2,1)}, s32[32,32,256]{2,1,0:T(8,128)}, s32[32,32,256]{2,1,0:T(8,128)}, ...), condition=%wide.region_1.2_spmd, body=%wide.region_0.1_spmd.sunk | while | flops 71565312 | bytes 1557069 | solution.py:30
  8.8 3.7 fusion.50
  14.8 3.7 fusion.50
  20.8 3.7 fusion.50
  26.8 3.7 fusion.50
  32.9 3.7 fusion.50
  38.9 3.7 fusion.50
  44.9 3.7 fusion.50
  51.0 3.7 fusion.50
  57.0 3.7 fusion.50
  63.0 3.7 fusion.50
  69.0 3.7 fusion.50
  75.1 3.7 fusion.50
  81.1 3.7 fusion.50
  87.1 3.7 fusion.50
  93.2 3.7 fusion.50
  99.2 3.7 fusion.50
  105.2 3.7 fusion.50
  111.2 3.7 fusion.50
  117.2 3.7 fusion.50
  123.3 3.7 fusion.50
  129.3 3.7 fusion.50
  135.3 3.7 fusion.50
  141.4 3.7 fusion.50
  147.4 3.7 fusion.50
  153.4 3.7 fusion.50
  159.4 3.7 fusion.50
  165.5 3.7 fusion.50
  171.5 3.7 fusion.50
  177.5 3.7 fusion.50
  183.6 3.7 fusion.50
  189.6 3.7 fusion.50
  195.6 3.7 fusion.50
  200.1 6.1 convolution_bitcast_fusion
  206.2 37.5 %reduce-scatter.3.cloned.1.call-done = f32[64,512]{1,0:T(8,128)} async-done(((f32[64,4096]{1,0:T(8,128)}), f32[64,512]{1,0:T(8,128)}) %reduce-scatter.3.cloned.1.call-update) | async-done | bytes 131088 | tf_op jit(solution)/shard_map/reduce_scatter | solution.py:55
  244.2 138.1 %psum.57 = f32[64,64]{1,0:T(8,128)S(1)} all-reduce(f32[64,64]{1,0:T(8,128)S(1)} %fusion.21), channel_id=1, replica_groups=mesh['pix'=32,'feat'=8] {'pix'}, use_global_device_ids=true, to_apply=%region_4.5 | all-reduce | flops 4096 | bytes 32768 | tf_op jit(solution)/shard_map/psum | solution.py:57
  382.2 23.6 %psum.58 = f32[64,64]{1,0:T(8,128)S(1)} all-reduce(f32[64,64]{1,0:T(8,128)S(1)} %psum.57), channel_id=1, replica_groups=mesh['pix'=32,'feat'=8] {'feat'}, use_global_device_ids=true, to_apply=%region_5.6 | all-reduce | flops 4096 | bytes 32768 | tf_op jit(solution)/shard_map/psum | solution.py:57
  407.0 13.1 %all_gather.6 = bf16[64,4096]{1,0:T(8,128)(2,1)S(1)} all-gather(bf16[64,512]{1,0:T(8,128)(2,1)S(1)} %get-tuple-element.42), channel_id=1, replica_groups=mesh['pix'=32,'feat'=8] {'feat'}, dimensions={1}, use_global_device_ids=true | all-gather | bytes 589824 | tf_op jit(solution)/shard_map/all_gather | solution.py:68
  420.1 6.0 convolution_multiply_fusion.1
  426.4 23.8 %psum.59 = f32[64,64]{1,0:T(8,128)S(1)} all-reduce(f32[64,64]{1,0:T(8,128)S(1)} %fusion.22), channel_id=1, replica_groups=mesh['pix'=32,'feat'=8] {'feat'}, use_global_device_ids=true, to_apply=%region_6.7 | all-reduce | flops 4096 | bytes 32768 | tf_op jit(solution)/shard_map/psum | solution.py:79
  450.6 6.0 fusion.16
  456.7 33.3 %reduce-scatter.5.cloned.1.call-done = f32[64,512]{1,0:T(8,128)} async-done(((f32[64,4096]{1,0:T(8,128)}), f32[64,512]{1,0:T(8,128)}) %reduce-scatter.5.cloned.1.call-update) | async-done | bytes 131088 | tf_op jit(solution)/shard_map/reduce_scatter | solution.py:55
  490.4 138.1 %psum.61 = f32[64,64]{1,0:T(8,128)S(1)} all-reduce(f32[64,64]{1,0:T(8,128)S(1)} %fusion.23), channel_id=1, replica_groups=mesh['pix'=32,'feat'=8] {'pix'}, use_global_device_ids=true, to_apply=%region_9.10 | all-reduce | flops 4096 | bytes 32768 | tf_op jit(solution)/shard_map/psum | solution.py:57
  628.5 23.8 %psum.62 = f32[64,64]{1,0:T(8,128)S(1)} all-reduce(f32[64,64]{1,0:T(8,128)S(1)} %psum.61), channel_id=1, replica_groups=mesh['pix'=32,'feat'=8] {'feat'}, use_global_device_ids=true, to_apply=%region_10.11 | all-reduce | flops 4096 | bytes 32768 | tf_op jit(solution)/shard_map/psum | solution.py:57
  652.3 1.2 fusion.20
  653.5 13.1 %all_gather.7 = bf16[64,4096]{1,0:T(8,128)(2,1)S(1)} all-gather(bf16[64,512]{1,0:T(8,128)(2,1)S(1)} %get-tuple-element.44), channel_id=1, replica_groups=mesh['pix'=32,'feat'=8] {'feat'}, dimensions={1}, use_global_device_ids=true | all-gather | bytes 589824 | tf_op jit(solution)/shard_map/all_gather | solution.py:68
  666.6 6.0 convolution_multiply_fusion
  672.9 23.8 %psum.63 = f32[64,64]{1,0:T(8,128)S(1)} all-reduce(f32[64,64]{1,0:T(8,128)S(1)} %fusion.24), channel_id=1, replica_groups=mesh['pix'=32,'feat'=8] {'feat'}, use_global_device_ids=true, to_apply=%region_11.12 | all-reduce | flops 4096 | bytes 32768 | tf_op jit(solution)/shard_map/psum | solution.py:79
  (152 shorter events, 79.7 us)
Async XLA Ops:
  7.2 236.6 %reduce-scatter.3.cloned.1.call-start = ((), (), s32[]{:S(2)}) async-start(), calls=%async_computation.2 | async-start | bytes 1179648 | tf_op jit(solution)/shard_map/reduce_scatter | solution.py:55
  7.2 192.9 %copy-start = (f32[1024,64]{0,1:T(8,128)S(1)}, f32[1024,64]{0,1:T(8,128)}, u32[]{:S(2)}) copy-start(f32[1024,64]{0,1:T(8,128)} %param.10) | copy-start | bytes 786436
  200.1 205.7 %copy-start.2 = (f32[64,512]{1,0:T(8,128)S(1)}, f32[64,512]{1,0:T(8,128)}, u32[]{:S(2)}) copy-start(f32[64,512]{1,0:T(8,128)} %param.11) | copy-start | bytes 393220
  206.2 199.6 %all-reduce.3.cloned.1.call-start = ((), (), s32[]{:S(2)}) async-start(), calls=%async_computation.3 | async-start | bytes 262144 | tf_op jit(solution)/shard_map/psum | solution.py:56
  243.8 246.3 %reduce-scatter.5.cloned.1.call-start = ((), (), s32[]{:S(2)}) async-start(), calls=%async_computation.4 | async-start | bytes 1179648 | tf_op jit(solution)/shard_map/reduce_scatter | solution.py:55
  456.7 195.6 %all-reduce.5.cloned.1.call-start = ((), (), s32[]{:S(2)}) async-start(), calls=%async_computation.5 | async-start | bytes 262144 | tf_op jit(solution)/shard_map/psum | solution.py:56
  653.5 44.3 %copy-start.1 = (f32[64,512]{1,0:T(8,128)}, f32[64,512]{1,0:T(8,128)S(1)}, u32[]{:S(2)}) copy-start(f32[64,512]{1,0:T(8,128)S(1)} %get-tuple-element.45) | copy-start | bytes 393220
Sparse Core Ops, SparseCore 0:
  206.3 37.3 reduce-scatter.2
  247.2 139.5 all-reduce.2
  456.8 33.1 reduce-scatter.4
  493.7 139.5 all-reduce.4
